TPU v7x, 32 devices: a whole 2x2x4 slice. The times are simulated.
32 devices in a mesh: sub: 8 (over z, x), coarse: 4 (over y, core).
Axes of the slice: x: 2, y: 2, z: 4, core: 2. Of those that a mesh axis runs over, the one named last changes fastest.
Arguments:
- residual: bfloat16 [128, 512, 256], P(('sub', 'coarse')), may hold values from -6 to 6
- margin: int32 [128, 4], P(('sub', 'coarse')), may hold values from 0 to 5, as said below
- inverse_blocks: bfloat16 [128, 4, 256, 256], P(('sub', 'coarse')), may hold values from -0.1875 to 0.1875
- interface: int32 [128, 2], P(('sub', 'coarse')), may hold values from 0 to 11, as said below
- basis: bfloat16 [128, 2, 256, 128], P(('sub', 'coarse')), may hold values from -0.375 to 0.375
- coarse_pattern: int32 [12, 4], P('coarse'), may hold values from 0 to 11, as said below
- coarse_inverse: bfloat16 [12, 4, 128, 128], P('coarse'), may hold values from -0.0546875 to 0.0546875
Outputs:
- correction: bfloat16 [128, 512, 256], P(('sub', 'coarse'))
Inputs may be any that keep to these rules, and one draw needn't show every extreme that they name: margin[j, 0] is j's own slot j % 4 + 1; the first block of each subdomain has slot 0 in entry 1 and the last has slot 5 in entry 2. interface[j, 0] = j % 12. coarse_pattern[n, 0] = n.
All inputs are finite; a program needn't handle non-finite values.
Results may differ from a plain program's by a relative error of at most 0.0051.
Values may be sent and summed in bfloat16 or wider, within the bound.
No kernel may reach another device: no remote copies, remote signals or barrier semaphores. Data moves between devices by JAX's collectives and lax.ppermute only.
A program may use at most 64 MiB of HBM per device.

v0:
```python
import jax
import jax.numpy as jnp
from jax import lax
from jax.sharding import PartitionSpec as P


def with_halo(cells, sides, width):
    for axis, dim in sides:
        count = lax.axis_size(axis)
        ends = count - 1
        head = lax.slice_in_dim(cells, 0, width, axis=dim)
        tail = lax.slice_in_dim(cells, cells.shape[dim] - width, cells.shape[dim], axis=dim)
        cells = jnp.concatenate(
            [
                lax.ppermute(tail, axis, [(i, (i + 1) % count) for i in range(ends)]),
                cells,
                lax.ppermute(head, axis, [((i + 1) % count, i) for i in range(ends)]),
            ],
            axis=dim,
        )
    return cells


def coarse_rows(inputs, coarse_pattern, coarse_inverse):
    chosen = jnp.take(inputs, coarse_pattern, axis=0)
    return jnp.einsum(
        "nerc,necd->nrd", chosen, coarse_inverse, preferred_element_type=jnp.float32
    ).astype(jnp.bfloat16)


def per_device(residual, margin, inverse_blocks, interface, basis, coarse_pattern, coarse_inverse):
    extended = with_halo(residual, ((("sub", "coarse"), 0),), 1)
    terms = jnp.einsum("jrb,jqbc->jqrc", residual, basis, preferred_element_type=jnp.float32)
    total_blocks = coarse_pattern.shape[0] * lax.axis_size("coarse")
    labels = jnp.arange(total_blocks, dtype=jnp.int32)
    onehot = (interface[:, :, None] == labels[None, None, :]).astype(jnp.float32)
    restricted = jnp.einsum("jqn,jqrc->nrc", onehot, terms, precision=lax.Precision.HIGHEST)
    picked = jnp.take(extended, margin, axis=0)
    local = jnp.einsum("jerb,jebc->jrc", picked, inverse_blocks, preferred_element_type=jnp.float32)
    shares = lax.psum_scatter(restricted, "coarse", scatter_dimension=0, tiled=True)
    shares = lax.psum(shares, "sub")
    inputs = lax.all_gather(shares.astype(jnp.bfloat16), "coarse", axis=0, tiled=True)
    owned = coarse_rows(inputs, coarse_pattern, coarse_inverse)
    coarse_out = lax.all_gather(owned, "coarse", axis=0, tiled=True)
    lifted = jnp.take(coarse_out, interface, axis=0)
    spread = jnp.einsum("jqrc,jqbc->jrb", lifted, basis, preferred_element_type=jnp.float32)
    return (local + spread).astype(jnp.bfloat16)


def solution(mesh):
    in_specs = (
        P(("sub", "coarse"), None, None),
        P(("sub", "coarse"), None),
        P(("sub", "coarse"), None, None, None),
        P(("sub", "coarse"), None),
        P(("sub", "coarse"), None, None, None),
        P("coarse", None),
        P("coarse", None, None, None),
    )
    out_specs = P(("sub", "coarse"), None, None)
    return jax.shard_map(
        per_device, mesh=mesh, in_specs=in_specs, out_specs=out_specs, check_vma=False
    )
```

profile of v0, /device:TPU:6, one launch (start us, length us, event | category | flops | bytes accessed | tf_op | source)
XLA Modules:
  0.0 169.5 jit_solution(14236015216186397533)
XLA Ops:
  6.5 0.0 copy-start
  6.5 0.0 reduce-scatter.2.cloned.1.call-start
  6.5 3.4 %convolution_bitcast_fusion.1 = f32[4,2,512,128]{2,3,1,0:T(8,128)} fusion(bf16[4,2,256,128]{3,2,1,0:T(8,128)(2,1)} %param.11, bf16[4,512,256]{2,1,0:T(8,128)(2,1)} %param.7), kind=kOutput, calls=%fused_computation.10 | convolution fusion | flops 268435456 | bytes 3670016 | tf_op jit(solution)/shard_map/jrb,jqbc->jqrc/dot_general | solution.py:33
  9.9 0.0 copy-start.4
  9.9 2.9 %copy.16 = f32[4,2,512,128]{3,0,1,2:T(4,128)} copy(f32[4,2,512,128]{2,3,1,0:T(8,128)} %convolution_bitcast_fusion.1) | data formatting | bytes 4194304 | tf_op jit(solution)/shard_map/jrb,jqbc->jqrc/transpose | solution.py:33
  12.8 0.0 copy-done.4
  12.8 4.1 %convolution_bitcast_fusion = f32[12,512,128]{2,0,1:T(8,128)S(1)} fusion(f32[4,2,512,128]{3,0,1,2:T(4,128)} %copy.16, s32[4,2]{0,1:T(2,128)S(1)} %copy-done.4), kind=kOutput, calls=%fused_computation.6 | convolution fusion | flops 75497568 | bytes 5242912 | tf_op jit(solution)/shard_map/jqn,jqrc->nrc/dot_general | solution.py:37
  17.0 2.6 %copy.17 = f32[12,512,128]{2,1,0:T(8,128)} copy(f32[12,512,128]{2,0,1:T(8,128)S(1)} %convolution_bitcast_fusion) | data formatting | bytes 6291456 | tf_op jit(solution)/shard_map/jqn,jqrc->nrc/dot_general | solution.py:37
  19.6 0.0 copy-start.2
  19.6 0.0 reduce-scatter.2.cloned.1.call-update
  19.6 0.0 all-gather.3.cloned.1.call-start
  19.6 38.3 %reduce-scatter.2.cloned.1.call-done = f32[3,512,128]{2,1,0:T(8,128)} async-done(((f32[12,512,128]{2,1,0:T(8,128)}), f32[3,512,128]{2,1,0:T(8,128)}) %reduce-scatter.2.cloned.1.call-update) | async-done | bytes 786448 | tf_op jit(solution)/shard_map/reduce_scatter | solution.py:40
  58.0 44.8 %all-reduce.1 = bf16[3,512,128]{2,1,0:T(8,128)(2,1)} all-reduce(f32[3,512,128]{2,1,0:T(8,128)} %reduce-scatter.2.cloned.1.call-done), channel_id=1, replica_groups=mesh['sub'=8,'coarse'=4] {'sub'}, use_global_device_ids=true, to_apply=%region_1.2 | all-reduce | flops 196608 | bytes 1179648 | tf_op jit(solution)/shard_map/psum | solution.py:41
  102.7 0.0 all-gather.3.cloned.1.call-update
  102.8 0.0 all-gather.5.cloned.1.call-start
  102.8 0.0 copy-done.2
  102.8 0.1 reshape.26
  102.9 19.7 %all-gather.3.cloned.1.call-done = bf16[12,512,128]{2,1,0:T(8,128)(2,1)} async-done(((bf16[3,512,128]{2,1,0:T(8,128)(2,1)}), bf16[12,512,128]{2,1,0:T(8,128)(2,1)}) %all-gather.3.cloned.1.call-update) | async-done | bytes 1572880 | tf_op jit(solution)/shard_map/all_gather | solution.py:42
  122.6 3.4 %gather_fusion.1 = bf16[12,512,128]{2,1,0:T(8,128)(2,1)} fusion(bf16[12,512,128]{2,1,0:T(8,128)(2,1)} %all-gather.3.cloned.1.call-done, s32[1024]{0:T(1024)S(1)} %pad_clamp_fusion.1), kind=kCustom, calls=%fused_computation.1 | custom fusion | bytes 3145776 | tf_op jit(solution)/shard_map/jit(_take)/gather | solution.py:25
  126.0 0.0 copy-start.1
  126.0 0.0 copy-start.3
  126.0 2.9 %fusion.13 = bf16[3,512,128]{2,1,0:T(8,128)(2,1)} fusion(bf16[3,4,128,128]{3,2,1,0:T(8,128)(2,1)} %param.13, bf16[3,4,512,128]{3,2,1,0:T(8,128)(2,1)} %bitcast.36, pred[3,4]{1,0:T(4,128)(4,1)S(1)} %compare_and_fusion), kind=kOutput, calls=%fused_computation.16 | convolution fusion | flops 202309632 | bytes 2359308 | tf_op jit(solution)/shard_map/nerc,necd->nrd/dot_general | solution.py:26
  128.9 0.0 all-gather.5.cloned.1.call-update
  128.9 0.0 copy-done.1
  128.9 0.8 fusion.28
  129.8 3.2 %collective-permute-start.1 = (bf16[1,512,256]{2,1,0:T(8,128)(2,1)}, bf16[1,512,256]{2,1,0:T(8,128)(2,1)S(1)}, u32[]{:S(2)}, u32[]{:S(2)}) collective-permute-start(bf16[1,512,256]{2,1,0:T(8,128)(2,1)} %get-tuple-element.6), channel_id=1, source_target_pairs={{1,0},{2,1},{3,2},{4,3},{5,4},{6,5},{7,6},{8,7},{9,8},{10,9},{11,1... | collective-permute-start | bytes 786440 | tf_op jit(solution)/shard_map/ppermute | solution.py:17
  133.0 1.9 %collective-permute-start = (bf16[1,512,256]{2,1,0:T(8,128)(2,1)}, bf16[1,512,256]{2,1,0:T(8,128)(2,1)}, u32[]{:S(2)}, u32[]{:S(2)}) collective-permute-start(bf16[1,512,256]{2,1,0:T(8,128)(2,1)} %get-tuple-element.5), channel_id=1, source_target_pairs={{0,1},{1,2},{2,3},{3,4},{4,5},{5,6},{6,7},{7,8},{8,9},{9,10},{10,1... | collective-permute-start | bytes 786440 | tf_op jit(solution)/shard_map/ppermute | solution.py:15
  134.9 0.1 copy.18
  135.0 0.1 reshape.34
  135.1 0.0 copy-done.3
  135.1 0.1 reshape.18
  135.2 0.1 copy.14
  135.4 1.9 %collective-permute-done.1 = bf16[1,512,256]{2,1,0:T(8,128)(2,1)S(1)} collective-permute-done((bf16[1,512,256]{2,1,0:T(8,128)(2,1)}, bf16[1,512,256]{2,1,0:T(8,128)(2,1)S(1)}, u32[]{:S(2)}, u32[]{:S(2)}) %collective-permute-start.1) | collective-permute-done | bytes 262176 | tf_op jit(solution)/shard_map/ppermute | solution.py:17
  137.2 11.0 %collective-permute-done = bf16[1,512,256]{2,1,0:T(8,128)(2,1)} collective-permute-done((bf16[1,512,256]{2,1,0:T(8,128)(2,1)}, bf16[1,512,256]{2,1,0:T(8,128)(2,1)}, u32[]{:S(2)}, u32[]{:S(2)}) %collective-permute-start) | collective-permute-done | bytes 262176 | tf_op jit(solution)/shard_map/ppermute | solution.py:15
  148.3 2.3 %pad_maximum_fusion = bf16[6,512,256]{2,1,0:T(8,128)(2,1)} fusion(bf16[1,512,256]{2,1,0:T(8,128)(2,1)S(1)} %collective-permute-done.1, bf16[4,512,256]{2,1,0:T(8,128)(2,1)S(1)} %copy-done.1, bf16[1,512,256]{2,1,0:T(8,128)(2,1)} %collective-permute-done), kind=kLoop, calls=%fused_computation.11 | loop fusion | flops 1572864 | bytes 3145728 | tf_op jit(solution)/shard_map/concatenate | solution.py:13
  150.6 4.2 %gather_fusion = bf16[16,512,256]{2,1,0:T(8,128)(2,1)} fusion(bf16[6,512,256]{2,1,0:T(8,128)(2,1)} %pad_maximum_fusion, s32[1024]{0:T(1024)S(1)} %pad_clamp_fusion.2), kind=kCustom, calls=%fused_computation | custom fusion | bytes 8388672 | tf_op jit(solution)/shard_map/jit(_take)/gather | solution.py:38
  154.8 0.0 all-gather.5.cloned.1.call-done
  154.8 2.2 %gather_fusion.2 = bf16[8,512,128]{2,1,0:T(8,128)(2,1)S(1)} fusion(bf16[12,512,128]{2,1,0:T(8,128)(2,1)} %all-gather.5.cloned.1.call-done, s32[1024]{0:T(1024)S(1)} %pad_clamp_fusion), kind=kCustom, calls=%fused_computation.2 | custom fusion | bytes 2097184 | tf_op jit(solution)/shard_map/jit(_take)/gather | solution.py:45
  156.9 1.5 fusion.17
  158.4 0.0 copy-done
  158.5 4.5 %fusion.3 = bf16[4,512,256]{2,1,0:T(8,128)(2,1)} fusion(f32[4,512,256,1]{2,1,3,0:T(8,128)S(1)} %fusion.17, bf16[4,4,256,256]{3,2,1,0:T(8,128)(2,1)S(1)} %copy-done, bf16[4,4,512,256]{3,2,1,0:T(8,128)(2,1)} %bitcast.34, pred[4,4]{1,0:T(4,128)(4,1)S(1)} %compare_and_fusion.2), kind=kOutput, calls=%fused_computation.8 | convolution fusion | flops 1076887552 | bytes 9437200 | tf_op jit(solution)/shard_map/jerb,jebc->jrc/dot_general | solution.py:39
  (9 shorter events, 0.1 us)
Async XLA Ops:
  6.5 151.9 %copy-start = (bf16[4,4,256,256]{3,2,1,0:T(8,128)(2,1)S(1)}, bf16[4,4,256,256]{3,2,1,0:T(8,128)(2,1)}, u32[]{:S(2)}) copy-start(bf16[4,4,256,256]{3,2,1,0:T(8,128)(2,1)} %param.9) | copy-start | bytes 6291460
  6.5 51.4 %reduce-scatter.2.cloned.1.call-start = ((), (), s32[]{:S(2)}) async-start(), calls=%async_computation.1 | async-start | bytes 3932160 | tf_op jit(solution)/shard_map/reduce_scatter | solution.py:40
  9.9 2.9 %copy-start.4 = (s32[4,2]{0,1:T(2,128)S(1)}, s32[4,2]{0,1:T(2,128)}, u32[]{:S(2)}) copy-start(s32[4,2]{0,1:T(2,128)} %param.10) | copy-start | bytes 100
  19.6 83.3 %copy-start.2 = (s32[3,4]{1,0:T(4,128)S(1)}, s32[3,4]{1,0:T(4,128)}, u32[]{:S(2)}) copy-start(s32[3,4]{1,0:T(4,128)} %param.12) | copy-start | bytes 148
  19.6 103.0 %all-gather.3.cloned.1.call-start = ((), (), s32[]{:S(2)}) async-start(), calls=%async_computation.2 | async-start | bytes 1966080 | tf_op jit(solution)/shard_map/all_gather | solution.py:42
  102.8 52.0 %all-gather.5.cloned.1.call-start = ((), (), s32[]{:S(2)}) async-start(), calls=%async_computation.3 | async-start | bytes 1966080 | tf_op jit(solution)/shard_map/all_gather | solution.py:44
  126.0 3.0 %copy-start.1 = (bf16[4,512,256]{2,1,0:T(8,128)(2,1)S(1)}, bf16[4,512,256]{2,1,0:T(8,128)(2,1)}, u32[]{:S(2)}) copy-start(bf16[4,512,256]{2,1,0:T(8,128)(2,1)} %param.7) | copy-start | bytes 3145732
  126.0 9.2 %copy-start.3 = (s32[4,4]{1,0:T(4,128)S(1)}, s32[4,4]{1,0:T(4,128)}, u32[]{:S(2)}) copy-start(s32[4,4]{1,0:T(4,128)} %param.8) | copy-start | bytes 196
  129.8 7.4 %collective-permute-start.1 = (bf16[1,512,256]{2,1,0:T(8,128)(2,1)}, bf16[1,512,256]{2,1,0:T(8,128)(2,1)S(1)}, u32[]{:S(2)}, u32[]{:S(2)}) collective-permute-start(bf16[1,512,256]{2,1,0:T(8,128)(2,1)} %get-tuple-element.6), channel_id=1, source_target_pairs={{1,0},{2,1},{3,2},{4,3},{5,4},{6,5},{7,6},{8,7},{9,8},{10,9},{11,1... | collective-permute-start | bytes 786440 | tf_op jit(solution)/shard_map/ppermute | solution.py:17
  133.0 15.3 %collective-permute-start = (bf16[1,512,256]{2,1,0:T(8,128)(2,1)}, bf16[1,512,256]{2,1,0:T(8,128)(2,1)}, u32[]{:S(2)}, u32[]{:S(2)}) collective-permute-start(bf16[1,512,256]{2,1,0:T(8,128)(2,1)} %get-tuple-element.5), channel_id=1, source_target_pairs={{0,1},{1,2},{2,3},{3,4},{4,5},{5,6},{6,7},{7,8},{8,9},{9,10},{10,1... | collective-permute-start | bytes 786440 | tf_op jit(solution)/shard_map/ppermute | solution.py:15
Sparse Core Ops, SparseCore 0:
  19.7 38.1 reduce-scatter.1
  102.9 19.6 all-gather.2
  129.0 23.5 all-gather.4
where the time goes:
time: 170 us; the launch traced here: 169 us
  waiting for transfers between devices  71 us (42%)
  blocking collectives  44.8 us (26%)
  local copies, waits for them, and re-layouts  16.5 us (10%)
  matrix products  16.4 us (10%)
  between operations  13.2 us (8%)
  starting transfers between devices  5.22 us (3%)
  other arithmetic  2.37 us (1%)
    psum x1, blocking collectives, per_device(): shares = lax.psum(shares, 'sub')  44.8 us
    reduce_scatter x1, waiting for transfers between devices, per_device(): lax.psum_scatter(restricted, 'coarse', scatter_dimension=0, tiled=True)  38.3 us
    all_gather x1, waiting for transfers between devices, per_device(): lax.all_gather(shares.astype(jnp.bfloat16), 'coarse', axis=0, tiled=True)  19.7 us
    ppermute x1, waiting for transfers between devices, with_halo(): lax.ppermute(tail, axis, [(i, (i + 1) % count) for i in range(ends)])  11 us
    dot_general x1, matrix products, per_device(): jnp.einsum('jerb,jebc->jrc', picked, inverse_blocks, preferred_element_ty...  4.48 us
    gather x1, local copies, waits for them, and re-layouts, per_device(): picked = jnp.take(extended, margin, axis=0)  4.18 us
    dot_general x1, matrix products, per_device(): jnp.einsum('jqn,jqrc->nrc', onehot, terms, precision=lax.Precision.HIGHEST)  4.12 us
  transfers between devices with their start and end apart: 5, of which 4 were waited for; matrix products, arithmetic and copies ran while one was open for 5% of the time, Pallas kernels for 0%

commit v1 on v0

--- a/solution.py
+++ b/solution.py
@@ -38,7 +38,7 @@
     picked = jnp.take(extended, margin, axis=0)
     local = jnp.einsum("jerb,jebc->jrc", picked, inverse_blocks, preferred_element_type=jnp.float32)
     shares = lax.psum_scatter(restricted, "coarse", scatter_dimension=0, tiled=True)
-    shares = lax.psum(shares, "sub")
+    shares = jnp.sum(lax.all_gather(shares, "sub"), axis=0)
     inputs = lax.all_gather(shares.astype(jnp.bfloat16), "coarse", axis=0, tiled=True)
     owned = coarse_rows(inputs, coarse_pattern, coarse_inverse)
     coarse_out = lax.all_gather(owned, "coarse", axis=0, tiled=True)

time: 170 us -> 229 us (1.35)
  waiting for transfers between devices: 71 us -> 171 us
  blocking collectives: 44.8 us -> 0 us
  other arithmetic: 2.37 us -> 6.33 us
    all_gather x0 -> x1, waiting for transfers between devices: none -> 101 us  [per_device(): shares = jnp.sum(lax.all_gather(shares, 'sub'), axis=0)]
    psum x1 -> x0, blocking collectives: 44.8 us -> none  [per_device(): shares = lax.psum(shares, 'sub')]
    reduce_sum x0 -> x1, other arithmetic: none -> 3.96 us  [per_device(): shares = jnp.sum(lax.all_gather(shares, 'sub'), axis=0)]
  transfers between devices with their start and end apart: 5 -> 6, of which waited for: 4 -> 5; matrix products, arithmetic and copies ran while one was open for 5% -> 3% of each run, Pallas kernels for 0% -> 0%
where the time goes in v1:
time: 229 us; the launch traced here: 228 us
  waiting for transfers between devices  171 us (75%)
  local copies, waits for them, and re-layouts  16.5 us (7%)
  matrix products  16.4 us (7%)
  between operations  13.2 us (6%)
  other arithmetic  6.33 us (3%)
  starting transfers between devices  5.26 us (2%)
    all_gather x1, waiting for transfers between devices, per_device(): shares = jnp.sum(lax.all_gather(shares, 'sub'), axis=0)  101 us
    reduce_scatter x1, waiting for transfers between devices, per_device(): lax.psum_scatter(restricted, 'coarse', scatter_dimension=0, tiled=True)  38.3 us
    all_gather x1, waiting for transfers between devices, per_device(): lax.all_gather(shares.astype(jnp.bfloat16), 'coarse', axis=0, tiled=True)  17.8 us
    ppermute x1, waiting for transfers between devices, with_halo(): lax.ppermute(tail, axis, [(i, (i + 1) % count) for i in range(ends)])  11 us
  transfers between devices with their start and end apart: 6, of which 5 were waited for; matrix products, arithmetic and copies ran while one was open for 3% of the time, Pallas kernels for 0%

profile of v1, /device:TPU:6, one launch (start us, length us, event | category | flops | bytes accessed | tf_op | source)
XLA Modules:
  0.0 228.3 jit_solution(11721621654937100813)
XLA Ops:
  6.5 0.0 copy-start
  6.5 0.0 reduce-scatter.2.cloned.1.call-start
  6.5 3.4 %convolution_bitcast_fusion.1 = f32[4,2,512,128]{2,3,1,0:T(8,128)} fusion(bf16[4,2,256,128]{3,2,1,0:T(8,128)(2,1)} %param.11, bf16[4,512,256]{2,1,0:T(8,128)(2,1)} %param.7), kind=kOutput, calls=%fused_computation.10 | convolution fusion | flops 268435456 | bytes 3670016 | tf_op jit(solution)/shard_map/jrb,jqbc->jqrc/dot_general | solution.py:33
  9.9 0.0 copy-start.4
  9.9 2.9 %copy.15 = f32[4,2,512,128]{3,0,1,2:T(4,128)} copy(f32[4,2,512,128]{2,3,1,0:T(8,128)} %convolution_bitcast_fusion.1) | data formatting | bytes 4194304 | tf_op jit(solution)/shard_map/jrb,jqbc->jqrc/transpose | solution.py:33
  12.8 0.0 copy-done.4
  12.8 4.1 %convolution_bitcast_fusion = f32[12,512,128]{2,0,1:T(8,128)S(1)} fusion(f32[4,2,512,128]{3,0,1,2:T(4,128)} %copy.15, s32[4,2]{0,1:T(2,128)S(1)} %copy-done.4), kind=kOutput, calls=%fused_computation.6 | convolution fusion | flops 75497568 | bytes 5242912 | tf_op jit(solution)/shard_map/jqn,jqrc->nrc/dot_general | solution.py:37
  17.0 2.6 %copy.16 = f32[12,512,128]{2,1,0:T(8,128)} copy(f32[12,512,128]{2,0,1:T(8,128)S(1)} %convolution_bitcast_fusion) | data formatting | bytes 6291456 | tf_op jit(solution)/shard_map/jqn,jqrc->nrc/dot_general | solution.py:37
  19.6 0.0 reduce-scatter.2.cloned.1.call-update
  19.6 0.0 all-gather.9.cloned.1.call-start
  19.6 38.3 %reduce-scatter.2.cloned.1.call-done = f32[3,512,128]{2,1,0:T(8,128)} async-done(((f32[12,512,128]{2,1,0:T(8,128)}), f32[3,512,128]{2,1,0:T(8,128)}) %reduce-scatter.2.cloned.1.call-update) | async-done | bytes 786448 | tf_op jit(solution)/shard_map/reduce_scatter | solution.py:40
  57.9 0.0 all-gather.9.cloned.1.call-update
  58.0 0.0 all-gather.5.cloned.1.call-start
  58.0 101.4 %all-gather.9.cloned.1.call-done = f32[24,512,128]{2,1,0:T(8,128)} async-done(((f32[3,512,128]{2,1,0:T(8,128)}), f32[24,512,128]{2,1,0:T(8,128)}) %all-gather.9.cloned.1.call-update) | async-done | bytes 6291472 | tf_op jit(solution)/shard_map/all_gather | solution.py:41
  159.4 0.0 copy-start.2
  159.4 4.0 %reduce_sum.9 = bf16[3,512,128]{2,1,0:T(8,128)(2,1)} reduce(f32[8,3,512,128]{3,2,1,0:T(8,128)} %bitcast.35, f32[]{:T(128)} %constant.43.clone.1), dimensions={0}, to_apply=%region_1.2 | reduce | flops 1376256 | bytes 6684676 | tf_op jit(solution)/shard_map/reduce_sum | solution.py:41
  163.4 0.0 all-gather.5.cloned.1.call-update
  163.4 0.0 all-gather.7.cloned.1.call-start
  163.5 0.0 copy-done.2
  163.5 0.1 reshape.26
  163.6 17.8 %all-gather.5.cloned.1.call-done = bf16[12,512,128]{2,1,0:T(8,128)(2,1)} async-done(((bf16[3,512,128]{2,1,0:T(8,128)(2,1)}), bf16[12,512,128]{2,1,0:T(8,128)(2,1)}) %all-gather.5.cloned.1.call-update) | async-done | bytes 1572880 | tf_op jit(solution)/shard_map/all_gather | solution.py:42
  181.4 3.3 %gather_fusion.1 = bf16[12,512,128]{2,1,0:T(8,128)(2,1)} fusion(bf16[12,512,128]{2,1,0:T(8,128)(2,1)} %all-gather.5.cloned.1.call-done, s32[1024]{0:T(1024)S(1)} %pad_clamp_fusion.1), kind=kCustom, calls=%fused_computation.1 | custom fusion | bytes 3145776 | tf_op jit(solution)/shard_map/jit(_take)/gather | solution.py:25
  184.8 0.0 copy-start.1
  184.8 0.0 copy-start.3
  184.8 2.9 %fusion.13 = bf16[3,512,128]{2,1,0:T(8,128)(2,1)} fusion(bf16[3,4,128,128]{3,2,1,0:T(8,128)(2,1)} %param.13, bf16[3,4,512,128]{3,2,1,0:T(8,128)(2,1)} %bitcast.38, pred[3,4]{1,0:T(4,128)(4,1)S(1)} %compare_and_fusion), kind=kOutput, calls=%fused_computation.16 | convolution fusion | flops 202309632 | bytes 2359308 | tf_op jit(solution)/shard_map/nerc,necd->nrd/dot_general | solution.py:26
  187.7 0.0 all-gather.7.cloned.1.call-update
  187.7 0.0 copy-done.1
  187.7 0.9 fusion.28
  188.6 3.2 %collective-permute-start.1 = (bf16[1,512,256]{2,1,0:T(8,128)(2,1)}, bf16[1,512,256]{2,1,0:T(8,128)(2,1)S(1)}, u32[]{:S(2)}, u32[]{:S(2)}) collective-permute-start(bf16[1,512,256]{2,1,0:T(8,128)(2,1)} %get-tuple-element.6), channel_id=1, source_target_pairs={{1,0},{2,1},{3,2},{4,3},{5,4},{6,5},{7,6},{8,7},{9,8},{10,9},{11,1... | collective-permute-start | bytes 786440 | tf_op jit(solution)/shard_map/ppermute | solution.py:17
  191.8 1.9 collective-permute-start
  193.7 0.1 copy.17
  193.8 0.1 reshape.34
  193.9 0.0 copy-done.3
  193.9 0.1 reshape.18
  194.0 0.1 copy.13
  194.2 1.9 collective-permute-done.1
  196.0 11.0 %collective-permute-done = bf16[1,512,256]{2,1,0:T(8,128)(2,1)} collective-permute-done((bf16[1,512,256]{2,1,0:T(8,128)(2,1)}, bf16[1,512,256]{2,1,0:T(8,128)(2,1)}, u32[]{:S(2)}, u32[]{:S(2)}) %collective-permute-start) | collective-permute-done | bytes 262176 | tf_op jit(solution)/shard_map/ppermute | solution.py:15
  207.1 2.3 %pad_maximum_fusion = bf16[6,512,256]{2,1,0:T(8,128)(2,1)} fusion(bf16[1,512,256]{2,1,0:T(8,128)(2,1)S(1)} %collective-permute-done.1, bf16[4,512,256]{2,1,0:T(8,128)(2,1)S(1)} %copy-done.1, bf16[1,512,256]{2,1,0:T(8,128)(2,1)} %collective-permute-done), kind=kLoop, calls=%fused_computation.11 | loop fusion | flops 1572864 | bytes 3145728 | tf_op jit(solution)/shard_map/concatenate | solution.py:13
  209.4 4.2 %gather_fusion = bf16[16,512,256]{2,1,0:T(8,128)(2,1)} fusion(bf16[6,512,256]{2,1,0:T(8,128)(2,1)} %pad_maximum_fusion, s32[1024]{0:T(1024)S(1)} %pad_clamp_fusion.2), kind=kCustom, calls=%fused_computation | custom fusion | bytes 8388672 | tf_op jit(solution)/shard_map/jit(_take)/gather | solution.py:38
  213.6 0.0 all-gather.7.cloned.1.call-done
  213.6 2.2 gather_fusion.2
  215.7 1.5 fusion.17
  217.3 0.0 copy-done
  217.3 4.5 %fusion.3 = bf16[4,512,256]{2,1,0:T(8,128)(2,1)} fusion(f32[4,512,256,1]{2,1,3,0:T(8,128)S(1)} %fusion.17, bf16[4,4,256,256]{3,2,1,0:T(8,128)(2,1)S(1)} %copy-done, bf16[4,4,512,256]{3,2,1,0:T(8,128)(2,1)} %bitcast.36, pred[4,4]{1,0:T(4,128)(4,1)S(1)} %compare_and_fusion.2), kind=kOutput, calls=%fused_computation.8 | convolution fusion | flops 1076887552 | bytes 9437200 | tf_op jit(solution)/shard_map/jerb,jebc->jrc/dot_general | solution.py:39
  (9 shorter events, 0.1 us)
Async XLA Ops:
  6.5 210.7 %copy-start = (bf16[4,4,256,256]{3,2,1,0:T(8,128)(2,1)S(1)}, bf16[4,4,256,256]{3,2,1,0:T(8,128)(2,1)}, u32[]{:S(2)}) copy-start(bf16[4,4,256,256]{3,2,1,0:T(8,128)(2,1)} %param.9) | copy-start | bytes 6291460
  6.5 51.4 %reduce-scatter.2.cloned.1.call-start = ((), (), s32[]{:S(2)}) async-start(), calls=%async_computation.1 | async-start | bytes 3932160 | tf_op jit(solution)/shard_map/reduce_scatter | solution.py:40
  9.9 2.9 %copy-start.4 = (s32[4,2]{0,1:T(2,128)S(1)}, s32[4,2]{0,1:T(2,128)}, u32[]{:S(2)}) copy-start(s32[4,2]{0,1:T(2,128)} %param.10) | copy-start | bytes 100
  19.6 139.9 %all-gather.9.cloned.1.call-start = ((), (), s32[]{:S(2)}) async-start(), calls=%async_computation.4 | async-start | bytes 7077888 | tf_op jit(solution)/shard_map/all_gather | solution.py:41
  58.0 123.4 %all-gather.5.cloned.1.call-start = ((), (), s32[]{:S(2)}) async-start(), calls=%async_computation.2 | async-start | bytes 1966080 | tf_op jit(solution)/shard_map/all_gather | solution.py:42
  159.4 4.0 %copy-start.2 = (s32[3,4]{1,0:T(4,128)S(1)}, s32[3,4]{1,0:T(4,128)}, u32[]{:S(2)}) copy-start(s32[3,4]{1,0:T(4,128)} %param.12) | copy-start | bytes 148
  163.4 50.1 %all-gather.7.cloned.1.call-start = ((), (), s32[]{:S(2)}) async-start(), calls=%async_computation.3 | async-start | bytes 1966080 | tf_op jit(solution)/shard_map/all_gather | solution.py:44
  184.8 3.0 %copy-start.1 = (bf16[4,512,256]{2,1,0:T(8,128)(2,1)S(1)}, bf16[4,512,256]{2,1,0:T(8,128)(2,1)}, u32[]{:S(2)}) copy-start(bf16[4,512,256]{2,1,0:T(8,128)(2,1)} %param.7) | copy-start | bytes 3145732
  184.8 9.2 %copy-start.3 = (s32[4,4]{1,0:T(4,128)S(1)}, s32[4,4]{1,0:T(4,128)}, u32[]{:S(2)}) copy-start(s32[4,4]{1,0:T(4,128)} %param.8) | copy-start | bytes 196
  188.6 7.4 %collective-permute-start.1 = (bf16[1,512,256]{2,1,0:T(8,128)(2,1)}, bf16[1,512,256]{2,1,0:T(8,128)(2,1)S(1)}, u32[]{:S(2)}, u32[]{:S(2)}) collective-permute-start(bf16[1,512,256]{2,1,0:T(8,128)(2,1)} %get-tuple-element.6), channel_id=1, source_target_pairs={{1,0},{2,1},{3,2},{4,3},{5,4},{6,5},{7,6},{8,7},{9,8},{10,9},{11,1... | collective-permute-start | bytes 786440 | tf_op jit(solution)/shard_map/ppermute | solution.py:17
  191.8 15.3 %collective-permute-start = (bf16[1,512,256]{2,1,0:T(8,128)(2,1)}, bf16[1,512,256]{2,1,0:T(8,128)(2,1)}, u32[]{:S(2)}, u32[]{:S(2)}) collective-permute-start(bf16[1,512,256]{2,1,0:T(8,128)(2,1)} %get-tuple-element.5), channel_id=1, source_target_pairs={{0,1},{1,2},{2,3},{3,4},{4,5},{5,6},{6,7},{7,8},{8,9},{9,10},{10,1... | collective-permute-start | bytes 786440 | tf_op jit(solution)/shard_map/ppermute | solution.py:15
Sparse Core Ops, SparseCore 0:
  19.7 38.1 reduce-scatter.1
  60.4 99.0 all-gather.8
  163.5 17.8 all-gather.4
  187.8 23.5 all-gather.6
